TPU v7x, 512 devices: a whole 4x8x8 slice. The times are simulated.
512 devices in a mesh: group: 8 (over z_lo, core), dp: 8 (over y), tensor: 8 (over z_hi, x).
Axes of the slice: x: 4, y: 8, z: 8 (z_hi: 2, z_lo: 4; z = z_hi * 4 + z_lo), core: 2. Of those that a mesh axis runs over, the one named last changes fastest.
Arguments:
- keyvalue_local: float32 [8, 2, 4096, 1024], P('group', None, 'dp', 'tensor'), may hold values from -6 to 6
- keyvalue_anchor: float32 [2, 4096, 1024], P(None, 'dp', 'tensor'), may hold values from -6 to 6
- keyvalue_state: float32 [2, 4096, 1024], P(None, 'dp', 'tensor'), may hold values from -6 to 6
- router_local: float32 [8, 4096, 8], P('group', 'dp'), may hold values from -6 to 6
- router_anchor: float32 [4096, 8], P('dp'), may hold values from -6 to 6
- router_state: float32 [4096, 8], P('dp'), may hold values from -6 to 6
- gain_local: float32 [8, 2, 4096], P('group', None, 'dp'), may hold values from -6 to 6
- gain_anchor: float32 [2, 4096], P(None, 'dp'), may hold values from -6 to 6
- gain_state: float32 [2, 4096], P(None, 'dp'), may hold values from -6 to 6
- embed_local: float32 [8, 1000, 4096], P('group', 'dp', 'tensor'), may hold values from -6 to 6
- embed_anchor: float32 [1000, 4096], P('dp', 'tensor'), may hold values from -6 to 6
- embed_state: float32 [1000, 4096], P('dp', 'tensor'), may hold values from -6 to 6
- embed_basis: float32 [4096, 64], P('tensor'), may hold values from -0.25 to 0.25
- outer_rate: float32 [], replicated, may hold values from 0.5 to 1
Outputs:
- keyvalue_average: float32 [2, 4096, 1024], P(None, 'dp', 'tensor')
- keyvalue_momentum: float32 [2, 4096, 1024], P(None, 'dp', 'tensor')
- keyvalue_updated: float32 [2, 4096, 1024], P(None, 'dp', 'tensor')
- router_average: float32 [4096, 8], P('dp')
- router_momentum: float32 [4096, 8], P('dp')
- router_updated: float32 [4096, 8], P('dp')
- gain_average: float32 [2, 4096], P(None, 'dp')
- gain_momentum: float32 [2, 4096], P(None, 'dp')
- gain_updated: float32 [2, 4096], P(None, 'dp')
- embed_average: float32 [1000, 4096], P('dp', 'tensor')
- embed_momentum: float32 [1000, 4096], P('dp', 'tensor')
- embed_updated: float32 [1000, 4096], P('dp', 'tensor')
All inputs are finite; a program needn't handle non-finite values.
Results may differ from a plain program's by a relative error of at most 0.0001.
Values sent between devices are 32-bit elements; how exact they have to be, the bound alone decides.
No kernel may reach another device: no remote copies, remote signals or barrier semaphores. Data moves between devices by JAX's collectives and lax.ppermute only.
A program may use at most 64 MiB of HBM per device.

v0:
```python
import jax
import jax.numpy as jnp
from jax import lax
from jax.sharding import PartitionSpec as P

HIGHEST = lax.Precision.HIGHEST
MODE = "separate"


def nesterov(average, state, anchor, outer_rate):
    momentum = 0.5 * state + average
    updated = anchor - outer_rate * (average + 0.5 * momentum)
    return (average, momentum, updated)


def local(
    kv_local,
    kv_anchor,
    kv_state,
    r_local,
    r_anchor,
    r_state,
    g_local,
    g_anchor,
    g_state,
    e_local,
    e_anchor,
    e_state,
    basis,
    rate,
):
    groups = lax.axis_size("group")
    kv_diff = kv_anchor - kv_local[0]
    r_diff = r_anchor - r_local[0]
    g_diff = g_anchor - g_local[0]
    partial = jnp.dot(
        e_anchor - e_local[0], basis, precision=HIGHEST, preferred_element_type=jnp.float32
    )
    if MODE == "concat":
        partial = lax.psum(partial, "tensor")
        pieces = (kv_diff, r_diff, g_diff, partial)
        flat = jnp.concatenate([p.reshape(-1) for p in pieces])
        total = lax.psum(flat, "group")
        sums, at = ([], 0)
        for p in pieces:
            sums.append(total[at : at + p.size].reshape(p.shape))
            at += p.size
        kv_sum, r_sum, g_sum, factors = sums
    elif MODE == "separate":
        partial = lax.psum(partial, "tensor")
        kv_sum, r_sum, g_sum, factors = lax.psum((kv_diff, r_diff, g_diff, partial), "group")
    elif MODE == "nested":
        kv_sum, r_sum, g_sum = lax.psum((kv_diff, r_diff, g_diff), "group")
        factors = lax.psum(lax.psum(partial, "tensor"), "group")
    kv_out = nesterov(kv_sum / groups, kv_state, kv_anchor, rate)
    r_out = nesterov(r_sum / groups, r_state, r_anchor, rate)
    g_out = nesterov(g_sum / groups, g_state, g_anchor, rate)
    factors = factors / groups
    e_avg = jnp.dot(factors, basis.T, precision=HIGHEST, preferred_element_type=jnp.float32)
    e_out = nesterov(e_avg, e_state, e_anchor, rate)
    return (*kv_out, *r_out, *g_out, *e_out)


IN_SPECS = (
    P("group", None, "dp", "tensor"),
    P(None, "dp", "tensor"),
    P(None, "dp", "tensor"),
    P("group", "dp", None),
    P("dp", None),
    P("dp", None),
    P("group", None, "dp"),
    P(None, "dp"),
    P(None, "dp"),
    P("group", "dp", "tensor"),
    P("dp", "tensor"),
    P("dp", "tensor"),
    P("tensor", None),
    P(),
)
OUT_SPECS = (
    P(None, "dp", "tensor"),
    P(None, "dp", "tensor"),
    P(None, "dp", "tensor"),
    P("dp", None),
    P("dp", None),
    P("dp", None),
    P(None, "dp"),
    P(None, "dp"),
    P(None, "dp"),
    P("dp", "tensor"),
    P("dp", "tensor"),
    P("dp", "tensor"),
)


def solution(mesh):
    return jax.shard_map(local, mesh=mesh, in_specs=IN_SPECS, out_specs=OUT_SPECS, check_vma=False)
```

profile of v0, /device:TPU:32, one launch (start us, length us, event | category | flops | bytes accessed | tf_op | source)
XLA Modules:
  0.0 108.0 jit_solution(13273733922246938453)
XLA Ops:
  7.2 0.0 copy-start
  7.2 0.0 all-reduce.3.cloned.1.call-start
  7.2 2.1 %bitcast_subtract_fusion = f32[2,512,128]{2,1,0:T(8,128)} fusion(f32[2,512,128]{2,1,0:T(8,128)} %param.15, f32[1,2,512,128]{3,2,1,0:T(8,128)} %param.14), kind=kLoop, calls=%fused_computation | loop fusion | flops 131072 | bytes 1572864 | tf_op jit(solution)/shard_map/sub | solution.py:33
  9.3 0.0 copy-start.2
  9.3 0.0 copy-start.4
  9.3 0.0 all-reduce.3.cloned.1.call-update
  10.0 0.0 copy-done
  10.1 0.2 copy-done.2
  10.3 0.1 copy-done.4
  10.4 0.0 copy-start.6
  10.4 0.0 copy-start.7
  10.4 0.0 copy-start.8
  10.4 0.0 copy-start.10
  10.4 0.4 fusion
  10.7 0.0 copy-start.5
  10.8 58.1 %psum.38 = f32[125,64]{1,0:T(8,128)S(1)} all-reduce(f32[125,64]{1,0:T(8,128)S(1)} %fusion), channel_id=1, replica_groups=mesh['group'=8,'dp'=8,'tensor'=8] {'tensor'}, use_global_device_ids=true, to_apply=%region_3.0 | all-reduce | flops 8000 | bytes 64000 | tf_op jit(solution)/shard_map/psum | solution.py:50
  68.9 0.0 copy-done.6
  68.9 0.0 copy-done.7
  68.9 0.0 copy-done.8
  68.9 0.0 copy-done.10
  68.9 0.0 copy-start.11
  68.9 27.3 %all-reduce = (f32[512,8]{0,1:T(8,128)S(1)}, f32[2,512]{1,0:T(2,128)S(1)}, f32[125,64]{1,0:T(8,128)S(1)}) all-reduce(f32[512,8]{0,1:T(8,128)S(1)} %bitcast_subtract_fusion.3, f32[2,512]{1,0:T(2,128)S(1)} %bitcast_subtract_fusion.4, f32[125,64]{1,0:T(8,128)S(1)} %psum.38), channel_id=1, replica_groups=mesh['group'=8,'dp'=8,'tensor'=8] {'group'}, use_global_device_ids=true, to_apply=%region_1.0 | all-reduce | flops 13120 | bytes 104960 | tf_op jit(solution)/shard_map/psum | solution.py:51
  96.3 0.0 copy-start.9
  96.3 0.0 copy-done.11
  96.3 0.6 multiply_subtract_fusion.3
  96.9 0.1 copy-done.9
  97.0 0.6 multiply_subtract_fusion.2
  97.6 0.0 copy-done.5
  97.6 0.0 copy-start.1
  97.6 0.0 copy-start.3
  97.6 1.3 %multiply_subtract_fusion.1 = (f32[125,512]{1,0:T(8,128)}, f32[125,512]{1,0:T(8,128)}, f32[125,512]{1,0:T(8,128)}) fusion(f32[125,512]{1,0:T(8,128)S(1)} %copy-done.2, f32[]{:T(128)S(6)} %copy.32, f32[125,512]{1,0:T(8,128)S(1)} %copy-done.5, f32[512,64]{0,1:T(8,128)S(1)} %copy-done, f32[125,64]{1,0:T(8,128)S(1)} %get-tuple-element.14), kind=kOutput, calls=%fused_computation.6 | convolution fusion | flops 49544000 | bytes 1443076 | tf_op jit(solution)/shard_map/dot_general | solution.py:59
  98.9 0.0 all-reduce.3.cloned.1.call-done
  98.9 0.0 copy-done.1
  98.9 0.0 copy-done.3
  98.9 2.3 %multiply_subtract_fusion = (f32[2,512,128]{2,1,0:T(8,128)}, f32[2,512,128]{2,1,0:T(8,128)}, f32[2,512,128]{2,1,0:T(8,128)}) fusion(f32[2,512,128]{2,1,0:T(8,128)S(1)} %copy-done.1, f32[]{:T(128)S(6)} %copy.32, f32[2,512,128]{2,1,0:T(8,128)S(1)} %copy-done.3, f32[2,512,128]{2,1,0:T(8,128)} %all-reduce.3.cloned.1.call-done), kind=kLoop, calls=%fused_computation.1 | loop fusion | flops 917504 | bytes 3145732 | tf_op jit(solution)/shard_map/sub | solution.py:12
  (2 shorter events, 0.0 us)
Async XLA Ops:
  7.2 2.9 %copy-start = (f32[512,64]{0,1:T(8,128)S(1)}, f32[512,64]{0,1:T(8,128)}, u32[]{:S(2)}) copy-start(f32[512,64]{0,1:T(8,128)} %param.26) | copy-start | bytes 393220
  7.2 91.7 %all-reduce.3.cloned.1.call-start = ((), (), s32[]{:S(2)}) async-start(), calls=%async_computation | async-start | bytes 1048576 | tf_op jit(solution)/shard_map/psum | solution.py:51
  9.3 1.0 copy-start.2
  9.3 1.0 copy-start.4
  10.4 58.5 %copy-start.6 = (f32[512,8]{0,1:T(8,128)S(1)}, f32[512,8]{0,1:T(8,128)}, u32[]{:S(2)}) copy-start(f32[512,8]{0,1:T(8,128)} %param.18) | copy-start | bytes 49156
  10.4 58.5 %copy-start.7 = (f32[1,512,8]{1,2,0:T(8,128)S(1)}, f32[1,512,8]{1,2,0:T(8,128)}, u32[]{:S(2)}) copy-start(f32[1,512,8]{1,2,0:T(8,128)} %param.17) | copy-start | bytes 49156
  10.4 58.5 %copy-start.8 = (f32[2,512]{1,0:T(2,128)S(1)}, f32[2,512]{1,0:T(2,128)}, u32[]{:S(2)}) copy-start(f32[2,512]{1,0:T(2,128)} %param.21) | copy-start | bytes 12292
  10.4 58.5 %copy-start.10 = (f32[1,2,512]{2,1,0:T(2,128)S(1)}, f32[1,2,512]{2,1,0:T(2,128)}, u32[]{:S(2)}) copy-start(f32[1,2,512]{2,1,0:T(2,128)} %param.20) | copy-start | bytes 12292
  10.7 86.9 %copy-start.5 = (f32[125,512]{1,0:T(8,128)S(1)}, f32[125,512]{1,0:T(8,128)}, u32[]{:S(2)}) copy-start(f32[125,512]{1,0:T(8,128)} %param.25) | copy-start | bytes 768004
  68.9 27.3 %copy-start.11 = (f32[2,512]{1,0:T(2,128)S(1)}, f32[2,512]{1,0:T(2,128)}, u32[]{:S(2)}) copy-start(f32[2,512]{1,0:T(2,128)} %param.22) | copy-start | bytes 12292
  96.3 0.7 copy-start.9
  97.6 1.3 %copy-start.1 = (f32[2,512,128]{2,1,0:T(8,128)S(1)}, f32[2,512,128]{2,1,0:T(8,128)}, u32[]{:S(2)}) copy-start(f32[2,512,128]{2,1,0:T(8,128)} %param.15) | copy-start | bytes 1572868
  97.6 1.3 %copy-start.3 = (f32[2,512,128]{2,1,0:T(8,128)S(1)}, f32[2,512,128]{2,1,0:T(8,128)}, u32[]{:S(2)}) copy-start(f32[2,512,128]{2,1,0:T(8,128)} %param.16) | copy-start | bytes 1572868
Sparse Core Ops, SparseCore 0:
  11.5 82.3 all-reduce.2
where the time goes:
time: 108 us
  blocking collectives  85.4 us (79%)
  between operations  14.9 us (14%)
  other arithmetic  5.61 us (5%)
  matrix products  1.64 us (2%)
    psum x1, blocking collectives, local(): partial = lax.psum(partial, 'tensor')  58.1 us
    psum x1, blocking collectives, local(): lax.psum((kv_diff, r_diff, g_diff, partial), 'group')  27.3 us
    sub x3, other arithmetic, nesterov(): updated = anchor - outer_rate * (average + 0.5 * momentum)  3.52 us
  transfers between devices with their start and end apart: 1, of which 0 were waited for; matrix products, arithmetic and copies ran while one was open for 3% of the time, Pallas kernels for 0%

commit v1 on v0

--- a/solution.py
+++ b/solution.py
@@ -47,7 +47,8 @@
             at += p.size
         kv_sum, r_sum, g_sum, factors = sums
     elif MODE == "separate":
-        partial = lax.psum(partial, "tensor")
+        shards = lax.all_gather(partial, "tensor")
+        partial = jnp.sum(shards, axis=0)
         kv_sum, r_sum, g_sum, factors = lax.psum((kv_diff, r_diff, g_diff, partial), "group")
     elif MODE == "nested":
         kv_sum, r_sum, g_sum = lax.psum((kv_diff, r_diff, g_diff), "group")

time: 108 us -> 105 us (0.972)
  the two profiles are of different devices: /device:TPU:32 before, /device:TPU:2 now
where the time goes in v1:
time: 105 us; the launch traced here: 104 us
  blocking collectives  74.4 us (71%)
  between operations  14.9 us (14%)
  waiting for transfers between devices  7.08 us (7%)
  other arithmetic  5.64 us (5%)
  matrix products  1.73 us (2%)
    all_gather x1, blocking collectives, local(): shards = lax.all_gather(partial, 'tensor')  48 us
    psum x1, blocking collectives, local(): lax.psum((kv_diff, r_diff, g_diff, partial), 'group')  26.4 us
    psum x1, waiting for transfers between devices, local(): lax.psum((kv_diff, r_diff, g_diff, partial), 'group')  7.07 us
    sub x3, other arithmetic, nesterov(): updated = anchor - outer_rate * (average + 0.5 * momentum)  3.52 us
  transfers between devices with their start and end apart: 1, of which 1 were waited for; matrix products, arithmetic and copies ran while one was open for 3% of the time, Pallas kernels for 0%

profile of v1, /device:TPU:2, one launch (start us, length us, event | category | flops | bytes accessed | tf_op | source)
XLA Modules:
  0.0 104.2 jit_solution(14207348584325328699)
XLA Ops:
  7.2 0.0 copy-start
  7.2 0.0 all-reduce.3.cloned.1.call-start
  7.2 2.1 %bitcast_subtract_fusion = f32[2,512,128]{2,1,0:T(8,128)} fusion(f32[2,512,128]{2,1,0:T(8,128)} %param.15, f32[1,2,512,128]{3,2,1,0:T(8,128)} %param.14), kind=kLoop, calls=%fused_computation.1 | loop fusion | flops 131072 | bytes 1572864 | tf_op jit(solution)/shard_map/sub | solution.py:33
  9.3 0.0 copy-start.2
  9.3 0.0 copy-start.4
  9.3 0.0 all-reduce.3.cloned.1.call-update
  10.0 0.0 copy-done
  10.1 0.2 copy-done.2
  10.3 0.1 copy-done.4
  10.4 0.4 convolution_bitcast_fusion
  10.8 0.0 copy-start.6
  10.8 0.0 copy-start.7
  10.8 0.0 copy-start.8
  10.8 0.0 copy-start.10
  10.8 48.0 %all-gather.1 = f32[8,125,64]{1,2,0:T(8,128)S(1)} all-gather(f32[1,125,64]{1,2,0:T(8,128)S(1)} %convolution_bitcast_fusion), channel_id=2, replica_groups=mesh['group'=8,'dp'=8,'tensor'=8] {'tensor'}, dimensions={0}, use_global_device_ids=true | all-gather | bytes 288000 | tf_op jit(solution)/shard_map/all_gather | solution.py:50
  58.8 0.0 copy-done.6
  58.8 0.0 copy-done.7
  58.8 0.0 copy-start.5
  58.8 0.0 copy-done.8
  58.8 0.0 copy-done.10
  58.9 0.0 copy-start.11
  58.9 26.4 %all-reduce = (f32[512,8]{0,1:T(8,128)S(1)}, f32[2,512]{1,0:T(2,128)S(1)}, f32[125,64]{0,1:T(8,128)S(1)}) all-reduce(f32[512,8]{0,1:T(8,128)S(1)} %bitcast_subtract_fusion.3, f32[2,512]{1,0:T(2,128)S(1)} %bitcast_subtract_fusion.4, f32[125,64]{0,1:T(8,128)S(1)} %reduce_sum.9), channel_id=1, replica_groups=mesh['group'=8,'dp'=8,'tensor'=8] {'group'}, use_global_device_ids=true, to_apply=%region_1.0 | all-reduce | flops 13120 | bytes 104960 | tf_op jit(solution)/shard_map/psum | solution.py:52
  85.3 0.0 copy-start.9
  85.3 0.0 copy-done.11
  85.3 0.6 multiply_subtract_fusion.3
  85.9 0.1 copy-done.9
  86.0 0.6 multiply_subtract_fusion.2
  86.6 0.0 copy-done.5
  86.6 0.0 copy-start.1
  86.6 0.0 copy-start.3
  86.6 1.3 %multiply_subtract_fusion.1 = (f32[125,512]{1,0:T(8,128)}, f32[125,512]{1,0:T(8,128)}, f32[125,512]{1,0:T(8,128)}) fusion(f32[125,512]{1,0:T(8,128)S(1)} %copy-done.2, f32[]{:T(128)S(6)} %copy.32, f32[125,512]{1,0:T(8,128)S(1)} %copy-done.5, f32[512,64]{0,1:T(8,128)S(1)} %copy-done, f32[125,64]{0,1:T(8,128)S(1)} %get-tuple-element.14), kind=kOutput, calls=%fused_computation.6 | convolution fusion | flops 49544000 | bytes 1443076 | tf_op jit(solution)/shard_map/dot_general | solution.py:60
  88.0 7.1 %all-reduce.3.cloned.1.call-done = f32[2,512,128]{2,1,0:T(8,128)} async-done(((f32[2,512,128]{2,1,0:T(8,128)}), f32[2,512,128]{2,1,0:T(8,128)}) %all-reduce.3.cloned.1.call-update) | async-done | bytes 524304 | tf_op jit(solution)/shard_map/psum | solution.py:52
  95.0 0.0 copy-done.1
  95.0 0.0 copy-done.3
  95.0 2.3 %multiply_subtract_fusion = (f32[2,512,128]{2,1,0:T(8,128)}, f32[2,512,128]{2,1,0:T(8,128)}, f32[2,512,128]{2,1,0:T(8,128)}) fusion(f32[2,512,128]{2,1,0:T(8,128)S(1)} %copy-done.1, f32[]{:T(128)S(6)} %copy.32, f32[2,512,128]{2,1,0:T(8,128)S(1)} %copy-done.3, f32[2,512,128]{2,1,0:T(8,128)} %all-reduce.3.cloned.1.call-done), kind=kLoop, calls=%fused_computation.2 | loop fusion | flops 917504 | bytes 3145732 | tf_op jit(solution)/shard_map/sub | solution.py:12
  (3 shorter events, 0.0 us)
Async XLA Ops:
  7.2 2.9 %copy-start = (f32[512,64]{0,1:T(8,128)S(1)}, f32[512,64]{0,1:T(8,128)}, u32[]{:S(2)}) copy-start(f32[512,64]{0,1:T(8,128)} %param.26) | copy-start | bytes 393220
  7.2 87.8 %all-reduce.3.cloned.1.call-start = ((), (), s32[]{:S(2)}) async-start(), calls=%async_computation | async-start | bytes 1048576 | tf_op jit(solution)/shard_map/psum | solution.py:52
  9.3 1.0 copy-start.2
  9.3 1.0 copy-start.4
  10.8 48.1 %copy-start.6 = (f32[512,8]{0,1:T(8,128)S(1)}, f32[512,8]{0,1:T(8,128)}, u32[]{:S(2)}) copy-start(f32[512,8]{0,1:T(8,128)} %param.18) | copy-start | bytes 49156
  10.8 48.0 %copy-start.7 = (f32[1,512,8]{1,2,0:T(8,128)S(1)}, f32[1,512,8]{1,2,0:T(8,128)}, u32[]{:S(2)}) copy-start(f32[1,512,8]{1,2,0:T(8,128)} %param.17) | copy-start | bytes 49156
  10.8 48.1 %copy-start.8 = (f32[2,512]{1,0:T(2,128)S(1)}, f32[2,512]{1,0:T(2,128)}, u32[]{:S(2)}) copy-start(f32[2,512]{1,0:T(2,128)} %param.21) | copy-start | bytes 12292
  10.8 48.1 %copy-start.10 = (f32[1,2,512]{2,1,0:T(2,128)S(1)}, f32[1,2,512]{2,1,0:T(2,128)}, u32[]{:S(2)}) copy-start(f32[1,2,512]{2,1,0:T(2,128)} %param.20) | copy-start | bytes 12292
  58.8 27.8 %copy-start.5 = (f32[125,512]{1,0:T(8,128)S(1)}, f32[125,512]{1,0:T(8,128)}, u32[]{:S(2)}) copy-start(f32[125,512]{1,0:T(8,128)} %param.25) | copy-start | bytes 768004
  58.9 26.4 %copy-start.11 = (f32[2,512]{1,0:T(2,128)S(1)}, f32[2,512]{1,0:T(2,128)}, u32[]{:S(2)}) copy-start(f32[2,512]{1,0:T(2,128)} %param.22) | copy-start | bytes 12292
  85.3 0.7 copy-start.9
  86.6 8.4 %copy-start.1 = (f32[2,512,128]{2,1,0:T(8,128)S(1)}, f32[2,512,128]{2,1,0:T(8,128)}, u32[]{:S(2)}) copy-start(f32[2,512,128]{2,1,0:T(8,128)} %param.15) | copy-start | bytes 1572868
  86.6 8.4 %copy-start.3 = (f32[2,512,128]{2,1,0:T(8,128)S(1)}, f32[2,512,128]{2,1,0:T(8,128)}, u32[]{:S(2)}) copy-start(f32[2,512,128]{2,1,0:T(8,128)} %param.16) | copy-start | bytes 1572868
Sparse Core Ops, SparseCore 0:
  11.5 83.4 all-reduce.2
